TPU v7x, 512 devices: a whole 4x8x8 slice. The times are simulated.
512 devices in a mesh: row: 4 (over z_hi), col: 16 (over z_lo, x, core), chan: 8 (over y).
Axes of the slice: x: 4, y: 8, z: 8 (z_hi: 4, z_lo: 2; z = z_hi * 2 + z_lo), core: 2. Of those that a mesh axis runs over, the one named last changes fastest.
Arguments:
- snapshots: bfloat16 [8192, 2048], P('col', 'chan'), may hold values from -45 to 45
- offsets: int32 [4], replicated, may hold values from 0 to 15
- window_len: int32 [8192], replicated, may hold values from 64 to 256, as said below
- cone_exp: int32 [8192], replicated, may hold values from 0 to 3
Outputs:
- kernel: float32 [2048, 8192], P(('row', 'chan'), 'col')
Inputs may be any that keep to these rules, and one draw needn't show every extreme that they name: `window_len`: each value is a lag window length; at least one snapshot has a window of 256 lags.
All inputs are finite; a program needn't handle non-finite values.
Results may differ from a plain program's by a relative error of at most 0.0003.
Values may be sent and summed in bfloat16 or wider, within the bound.
No kernel may reach another device: no remote copies, remote signals or barrier semaphores. Data moves between devices by JAX's collectives and lax.ppermute only.
A program may use at most 64 MiB of HBM per device.

v0:
```python
import jax
import jax.numpy as jnp
from jax import lax
from jax.sharding import PartitionSpec as P

C = 2048
LAGS = 256
epsilon = 1e-05


def shifted(block, axis, distance):
    devices = range(lax.axis_size(axis))
    route = [((i - distance) % len(devices), i) for i in devices]
    return lax.ppermute(block, axis, route)


def spread(value, axis, source):
    kept = jnp.where(lax.axis_index(axis) == source, value, 0).astype(value.dtype)
    return lax.psum(kept, axis)


def power_int(frac, exps):
    square = frac * frac
    return jnp.where(
        exps == 0,
        jnp.ones_like(frac),
        jnp.where(exps == 1, frac, jnp.where(exps == 2, square, square * frac)),
    )


def cone_matrix(lengths, exps, lags):
    rows = lengths.shape[0]
    row_pos = lax.broadcasted_iota(jnp.int32, (rows, rows + lags - 1), 0)
    col_pos = lax.broadcasted_iota(jnp.int32, (rows, rows + lags - 1), 1)
    lag = row_pos + (lags - 1) - col_pos
    span = lengths[:, None]
    valid = (lag >= 0) & (lag < span)
    frac = (span.astype(jnp.float32) - lag.astype(jnp.float32)) / span.astype(jnp.float32)
    cone = jnp.where(valid, power_int(frac, exps[:, None]), jnp.zeros_like(frac))
    return cone / jnp.sum(cone, axis=1, keepdims=True)


def lag_sum(weights, dist, count):
    depth = dist.shape[0]
    width = dist.shape[1]
    columns = width - (depth - count)
    padded = jnp.pad(dist, ((0, 0), (count - 1, 0)))
    stride = width + count - 1
    flat = jnp.pad(padded.reshape(-1), (0, depth))
    skewed = flat.reshape(depth, stride + 1)[:, : columns + count - 1]
    diagonal = jnp.dot(
        weights, skewed, precision=lax.Precision.HIGHEST, preferred_element_type=jnp.float32
    )
    lined = diagonal.reshape(-1)[count - 1 : count - 1 + count * (columns + count - 2)]
    return lined.reshape(count, columns + count - 2)[:, :columns]


def shards(snapshots, offsets, window_len, cone_exp):
    block = snapshots.shape[0]
    lags = LAGS
    tail = snapshots[block - (lags - 1) :]
    history = shifted(tail, "col", 1)
    col_ext = jnp.concatenate([history, snapshots], axis=0)
    chosen = lax.dynamic_index_in_dim(offsets, lax.axis_index("row"), 0, keepdims=False)
    row_ext = spread(col_ext, "col", chosen)
    row_begin = chosen * block
    col_begin = lax.axis_index("col") * block
    row_weights = cone_matrix(
        lax.dynamic_slice_in_dim(window_len, row_begin, block),
        lax.dynamic_slice_in_dim(cone_exp, row_begin, block),
        lags,
    )
    col_weights = cone_matrix(
        lax.dynamic_slice_in_dim(window_len, col_begin, block),
        lax.dynamic_slice_in_dim(cone_exp, col_begin, block),
        lags,
    )
    share = block // lax.axis_size("chan")
    first = lax.axis_index("chan") * share
    mine = lax.dynamic_slice(row_weights, (first, first), (share, share + lags - 1))
    row_wide = row_ext.astype(jnp.float32)
    col_wide = col_ext.astype(jnp.float32)
    row_part = jnp.sum(row_wide * row_wide, axis=1)
    col_part = jnp.sum(col_wide * col_wide, axis=1)
    inner = jnp.dot(row_ext, col_ext.T, preferred_element_type=jnp.float32)
    dist = row_part[:, None] + col_part[None, :] - 2.0 * inner
    total = lax.psum_scatter(
        lag_sum(row_weights, dist, lax.axis_size("chan") * share),
        "chan",
        scatter_dimension=0,
        tiled=True,
    )
    row_full, col_norms = lax.psum((row_part, col_part), "chan")
    row_near = lax.dynamic_slice_in_dim(row_full, first, share + lags - 1)
    row_scale = jnp.sqrt(
        jnp.dot(mine, row_near, precision=lax.Precision.HIGHEST, preferred_element_type=jnp.float32)
        / C
        + epsilon
    )
    col_scale = jnp.sqrt(
        jnp.dot(
            col_weights,
            col_norms,
            precision=lax.Precision.HIGHEST,
            preferred_element_type=jnp.float32,
        )
        / C
        + epsilon
    )
    return jnp.exp(-total / (2.0 * C * row_scale[:, None] * col_scale[None, :]))


def solution(mesh):
    in_specs = (P("col", "chan"), P(), P(), P())
    out_specs = P(("row", "chan"), "col")
    return jax.shard_map(shards, mesh=mesh, in_specs=in_specs, out_specs=out_specs, check_vma=False)
```

profile of v0, /device:TPU:2, one launch (start us, length us, event | category | flops | bytes accessed | tf_op | source)
XLA Modules:
  0.0 241.1 jit_solution(13446755895322598838)
XLA Ops:
  6.5 0.0 copy-start
  6.5 0.0 all-reduce.5.cloned.1.call-start
  6.5 1.0 slice.12
  7.5 1.9 collective-permute-start
  9.5 1.2 dynamic_slice.22
  11.4 0.8 dynamic-slice_compare_fusion.5
  12.8 0.8 fusion.31
  13.6 0.2 collective-permute-done
  13.8 1.8 broadcast_select_fusion
  15.6 0.0 all-reduce.5.cloned.1.call-update
  15.7 0.0 reduce-scatter.2.cloned.1.call-start
  15.7 2.5 %fusion.21 = (f32[512]{0:T(512)S(1)}, f32[512]{0:T(512)S(1)}) fusion(pred[512]{0:T(512)(128)(4,1)S(1)} %get-tuple-element.17, f32[512]{0:T(512)S(1)} %get-tuple-element.19, pred[512]{0:T(512)(128)(4,1)S(1)} %get-tuple-element.16, pred[512]{0:T(512)(128)(4,1)S(1)} %get-tuple-element.18, s32[512]{0:T(512)S(1)} %get-tuple-element.20, ...), kind=kLoop, calls=%fused_computation.28 | loop fusion | flops 9816576 | bytes 17408 | tf_op jit(solution)/shard_map/reduce_sum | solution.py:40
  18.2 0.0 copy-done
  18.2 0.2 multiply_reduce_fusion
  18.4 127.8 %all-reduce.5.cloned.1.call-done = bf16[767,256]{1,0:T(8,128)(2,1)} async-done(((bf16[767,256]{1,0:T(8,128)(2,1)}), bf16[767,256]{1,0:T(8,128)(2,1)}) %all-reduce.5.cloned.1.call-update) | async-done | bytes 392720 | tf_op jit(solution)/shard_map/psum | solution.py:19
  146.2 1.2 multiply_reduce_fusion.1
  147.4 1.5 multiply_subtract_fusion
  148.9 2.7 %pad.8 = f32[767,1278]{1,0:T(8,128)} pad(f32[767,767]{1,0:T(8,128)S(1)} %multiply_subtract_fusion, f32[]{:T(128)} %constant.14.clone.1), padding=0_0x511_0 | pad | bytes 6274064 | tf_op jit(solution)/shard_map/jit(_pad)/pad | solution.py:47
  151.7 5.5 %reshape.37 = f32[980226]{0:T(1024)} reshape(f32[767,1278]{1,0:T(8,128)} %pad.8) | data formatting | bytes 7841808 | tf_op jit(solution)/shard_map/reshape | solution.py:49
  157.1 4.3 %pad.9 = f32[980993]{0:T(1024)} pad(f32[980226]{0:T(1024)} %reshape.37, f32[]{:T(128)} %constant.14.clone.1), padding=0_767 | pad | bytes 7844880 | tf_op jit(solution)/shard_map/jit(_pad)/pad | solution.py:49
  161.4 7.8 %reshape.38 = f32[767,1279]{1,0:T(8,128)} reshape(f32[980993]{0:T(1024)} %pad.9) | data formatting | bytes 7847944 | tf_op jit(solution)/shard_map/reshape | solution.py:50
  169.2 9.2 %fusion = f32[512,1023]{1,0:T(8,128)} fusion(f32[767,1279]{1,0:T(8,128)} %reshape.38, f32[512]{0:T(512)S(1)} %get-tuple-element.6, pred[512]{0:T(512)(128)(4,1)S(1)} %get-tuple-element.15, f32[512]{0:T(512)S(1)} %get-tuple-element.9, pred[512]{0:T(512)(128)(4,1)S(1)} %get-tuple-element.14, pred[512]{0:T(512)(128)(4,1)S(1)} %get-tuple-element.13, ...), kind=kOutput, calls=%fused_computation | convolution fusion | flops 4826332160 | bytes 5250560 | tf_op jit(solution)/shard_map/dot_general | solution.py:51
  178.4 2.9 %reshape.39 = f32[523776]{0:T(1024)S(1)} reshape(f32[512,1023]{1,0:T(8,128)} %fusion) | data formatting | bytes 4190208 | tf_op jit(solution)/shard_map/reshape | solution.py:54
  181.4 2.0 slice.17
  183.3 3.4 %reshape.40 = f32[512,1022]{1,0:T(8,128)S(1)} reshape(f32[523264]{0:T(1024)} %slice.17) | data formatting | bytes 4186112 | tf_op jit(solution)/shard_map/reshape | solution.py:55
  186.7 1.1 slice.18
  187.8 0.0 reduce-scatter.2.cloned.1.call-update
  187.8 0.9 broadcast_divide_fusion
  188.7 16.4 %all-reduce.2 = (f32[767]{0:T(1024)S(1)}, f32[767]{0:T(1024)S(1)}) all-reduce(f32[767]{0:T(1024)S(1)} %multiply_reduce_fusion, f32[767]{0:T(1024)S(1)} %multiply_reduce_fusion.1), channel_id=1, replica_groups=mesh['row'=4,'col'=16,'chan'=8] {'chan'}, use_global_device_ids=true, to_apply=%region_7.8 | all-reduce | flops 1534 | bytes 12272 | tf_op jit(solution)/shard_map/psum | solution.py:93
  205.1 0.1 dynamic_slice.26
  205.2 0.3 fusion.18
  205.5 2.5 %fusion.13 = f32[1,512]{1,0:T(1,128)S(1)} fusion(f32[767,1]{0,1:T(1,128)S(1)} %reshape.43, f32[512]{0:T(512)S(1)} %get-tuple-element.5, f32[512]{0:T(512)S(1)} %get-tuple-element.19, s32[512]{0:T(512)S(1)} %get-tuple-element.20, s32[512]{0:T(512)S(1)} %get-tuple-element.21, pred[512]{0:T(512)(128)(4,1)S(1)} %get-tuple-element.17, ...), kind=kOutput, calls=%fused_computation.17 | convolution fusion | flops 10210304 | bytes 14844 | tf_op jit(solution)/shard_map/dot_general | solution.py:101
  208.0 24.6 %reduce-scatter.2.cloned.1.call-done = f32[64,512]{1,0:T(8,128)} async-done(((f32[512,512]{1,0:T(8,128)}), f32[64,512]{1,0:T(8,128)}) %reduce-scatter.2.cloned.1.call-update) | async-done | bytes 131088 | tf_op jit(solution)/shard_map/reduce_scatter | solution.py:87
  232.5 1.7 divide_exponential_fusion
  (3 shorter events, 0.0 us)
Async XLA Ops:
  6.5 11.7 %copy-start = (bf16[512,256]{1,0:T(8,128)(2,1)S(1)}, bf16[512,256]{1,0:T(8,128)(2,1)}, u32[]{:S(2)}) copy-start(bf16[512,256]{1,0:T(8,128)(2,1)} %param.4) | copy-start | bytes 786436
  6.5 139.7 %all-reduce.5.cloned.1.call-start = ((), (), s32[]{:S(2)}) async-start(), calls=%async_computation.1 | async-start | bytes 786432 | tf_op jit(solution)/shard_map/psum | solution.py:19
  7.5 6.3 %collective-permute-start = (bf16[255,256]{1,0:T(8,128)(2,1)S(1)}, bf16[255,256]{1,0:T(8,128)(2,1)S(1)}, u32[]{:S(2)}, u32[]{:S(2)}) collective-permute-start(bf16[255,256]{1,0:T(8,128)(2,1)S(1)} %slice.12), channel_id=1, source_target_pairs={{120,0},{0,8},{8,16},{16,24},{24,32},{32,40},{40,48},{48,56},{56,6... | collective-permute-start | bytes 391688 | tf_op jit(solution)/shard_map/ppermute | solution.py:14
  15.7 216.9 %reduce-scatter.2.cloned.1.call-start = ((), (), s32[]{:S(2)}) async-start(), calls=%async_computation.2 | async-start | bytes 1179648 | tf_op jit(solution)/shard_map/reduce_scatter | solution.py:87
Sparse Core Ops, SparseCore 0:
  15.8 130.3 all-reduce.4
  187.9 44.5 reduce-scatter.1
where the time goes:
time: 242 us; the launch traced here: 241 us
  waiting for transfers between devices  153 us (63%)
  local copies, waits for them, and re-layouts  32 us (13%)
  blocking collectives  16.4 us (7%)
  between operations  14.8 us (6%)
  matrix products  13.5 us (6%)
  other arithmetic  9.83 us (4%)
    psum x1, waiting for transfers between devices, spread(): return lax.psum(kept, axis)  128 us
    reduce_scatter x1, waiting for transfers between devices, shards(): lax.psum_scatter(lag_sum(row_weights, dist, lax.axis_size('chan') * share...  24.6 us
    psum x1, blocking collectives, shards(): row_full, col_norms = lax.psum((row_part, col_part), 'chan')  16.4 us
    dot_general x1, matrix products, lag_sum(): jnp.dot(weights, skewed, precision=lax.Precision.HIGHEST, preferred_eleme...  9.22 us
    reshape x1, local copies, waits for them, and re-layouts, lag_sum(): skewed = flat.reshape(depth, stride + 1)[:, :columns + count - 1]  7.81 us
    reshape x1, local copies, waits for them, and re-layouts, lag_sum(): flat = jnp.pad(padded.reshape(-1), (0, depth))  5.49 us
  transfers between devices with their start and end apart: 3, of which 3 were waited for; matrix products, arithmetic and copies ran while one was open for 4% of the time, Pallas kernels for 0%

commit v1 on v0

--- a/solution.py
+++ b/solution.py
@@ -16,7 +16,7 @@
 
 def spread(value, axis, source):
     kept = jnp.where(lax.axis_index(axis) == source, value, 0).astype(value.dtype)
-    return lax.psum(kept, axis)
+    return jnp.sum(lax.all_gather(kept, axis), axis=0)
 
 
 def power_int(frac, exps):

time: 242 us -> 163 us (0.67)
  waiting for transfers between devices: 153 us -> 71 us
  other arithmetic: 9.83 us -> 12.7 us
    psum x1 -> x0, waiting for transfers between devices: 128 us -> none  [spread(): return lax.psum(kept, axis)]
    all_gather x0 -> x1, waiting for transfers between devices: none -> 47.3 us  [spread(): return jnp.sum(lax.all_gather(kept, axis), axis=0)]
    reduce_sum x0 -> x1, other arithmetic: none -> 3.85 us  [spread(): return jnp.sum(lax.all_gather(kept, axis), axis=0)]
    reduce_scatter x1, waiting for transfers between devices: 24.6 us -> 21.2 us  [shards(): lax.psum_scatter(lag_sum(row_weights, dist, lax.axis_size('chan') * share...]
  transfers between devices with their start and end apart: 3 -> 3, of which waited for: 3 -> 3; matrix products, arithmetic and copies ran while one was open for 4% -> 6% of each run, Pallas kernels for 0% -> 0%
where the time goes in v1:
time: 163 us; the launch traced here: 162 us
  waiting for transfers between devices  71 us (44%)
  local copies, waits for them, and re-layouts  32 us (20%)
  blocking collectives  17.2 us (11%)
  between operations  14.8 us (9%)
  other arithmetic  12.7 us (8%)
  matrix products  12.5 us (8%)
  starting transfers between devices  1.96 us (1%)
    all_gather x1, waiting for transfers between devices, spread(): return jnp.sum(lax.all_gather(kept, axis), axis=0)  47.3 us
    reduce_scatter x1, waiting for transfers between devices, shards(): lax.psum_scatter(lag_sum(row_weights, dist, lax.axis_size('chan') * share...  21.2 us
    psum x1, blocking collectives, shards(): row_full, col_norms = lax.psum((row_part, col_part), 'chan')  17.2 us
    dot_general x1, matrix products, lag_sum(): jnp.dot(weights, skewed, precision=lax.Precision.HIGHEST, preferred_eleme...  9.22 us
    reshape x1, local copies, waits for them, and re-layouts, lag_sum(): skewed = flat.reshape(depth, stride + 1)[:, :columns + count - 1]  7.81 us
    reshape x1, local copies, waits for them, and re-layouts, lag_sum(): flat = jnp.pad(padded.reshape(-1), (0, depth))  5.49 us
    pad x1, local copies, waits for them, and re-layouts, lag_sum(): flat = jnp.pad(padded.reshape(-1), (0, depth))  4.26 us
    reduce_sum x1, other arithmetic, spread(): return jnp.sum(lax.all_gather(kept, axis), axis=0)  3.85 us
  transfers between devices with their start and end apart: 3, of which 3 were waited for; matrix products, arithmetic and copies ran while one was open for 6% of the time, Pallas kernels for 0%

profile of v1, /device:TPU:2, one launch (start us, length us, event | category | flops | bytes accessed | tf_op | source)
XLA Modules:
  0.0 162.1 jit_solution(15728369632697735857)
XLA Ops:
  6.5 0.0 copy-start
  6.5 0.0 all-gather.2.cloned.1.call-start
  6.5 1.0 slice.12
  7.5 1.9 %collective-permute-start = (bf16[255,256]{1,0:T(8,128)(2,1)S(1)}, bf16[255,256]{1,0:T(8,128)(2,1)S(1)}, u32[]{:S(2)}, u32[]{:S(2)}) collective-permute-start(bf16[255,256]{1,0:T(8,128)(2,1)S(1)} %slice.12), channel_id=1, source_target_pairs={{120,0},{0,8},{8,16},{16,24},{24,32},{32,40},{40,48},{48,56},{56,6... | collective-permute-start | bytes 391688 | tf_op jit(solution)/shard_map/ppermute | solution.py:14
  9.5 1.2 dynamic_slice.22
  11.4 2.5 %collective-permute-done = bf16[255,256]{1,0:T(8,128)(2,1)S(1)} collective-permute-done((bf16[255,256]{1,0:T(8,128)(2,1)S(1)}, bf16[255,256]{1,0:T(8,128)(2,1)S(1)}, u32[]{:S(2)}, u32[]{:S(2)}) %collective-permute-start) | collective-permute-done | bytes 130592 | tf_op jit(solution)/shard_map/ppermute | solution.py:14
  13.8 1.8 %maximum_select_fusion = bf16[1,767,256]{2,1,0:T(8,128)(2,1)} fusion(bf16[1,512,256]{2,1,0:T(8,128)(2,1)} %bitcast.17, bf16[1,255,256]{2,1,0:T(8,128)(2,1)S(1)} %bitcast.18, pred[]{:T(512)S(6)} %eq.30), kind=kLoop, calls=%fused_computation.30 | loop fusion | flops 981760 | bytes 785409 | tf_op jit(solution)/shard_map/jit(_where)/select_n | solution.py:18
  15.7 0.0 all-gather.2.cloned.1.call-update
  15.7 0.0 reduce-scatter.2.cloned.1.call-start
  16.4 0.8 dynamic-slice_compare_fusion.5
  17.2 0.8 fusion.31
  18.0 2.5 %fusion.21 = (f32[512]{0:T(512)S(1)}, f32[512]{0:T(512)S(1)}) fusion(pred[512]{0:T(512)(128)(4,1)S(1)} %get-tuple-element.17, f32[512]{0:T(512)S(1)} %get-tuple-element.19, pred[512]{0:T(512)(128)(4,1)S(1)} %get-tuple-element.16, pred[512]{0:T(512)(128)(4,1)S(1)} %get-tuple-element.18, s32[512]{0:T(512)S(1)} %get-tuple-element.20, ...), kind=kLoop, calls=%fused_computation.28 | loop fusion | flops 9816576 | bytes 17408 | tf_op jit(solution)/shard_map/reduce_sum | solution.py:40
  20.4 0.0 copy-done
  20.4 0.2 multiply_reduce_fusion
  20.6 47.3 %all-gather.2.cloned.1.call-done = bf16[16,767,256]{2,1,0:T(8,128)(2,1)} async-done(((bf16[1,767,256]{2,1,0:T(8,128)(2,1)}), bf16[16,767,256]{2,1,0:T(8,128)(2,1)}) %all-gather.2.cloned.1.call-update) | async-done | bytes 6283280 | tf_op jit(solution)/shard_map/all_gather | solution.py:19
  68.0 3.9 %reduce_sum.49 = bf16[767,256]{1,0:T(8,128)(2,1)S(1)} reduce(bf16[16,767,256]{2,1,0:T(8,128)(2,1)} %all-gather.2.cloned.1.call-done, bf16[]{:T(256)} %constant.17.clone.1), dimensions={0}, to_apply=%region_1.2 | reduce | flops 2945280 | bytes 6675970 | tf_op jit(solution)/shard_map/reduce_sum | solution.py:19
  71.8 0.2 multiply_reduce_fusion.1
  72.0 0.5 multiply_subtract_fusion
  72.5 2.7 %pad.8 = f32[767,1278]{1,0:T(8,128)} pad(f32[767,767]{1,0:T(8,128)S(1)} %multiply_subtract_fusion, f32[]{:T(128)} %constant.15.clone.1), padding=0_0x511_0 | pad | bytes 6274064 | tf_op jit(solution)/shard_map/jit(_pad)/pad | solution.py:47
  75.3 5.5 %reshape.66 = f32[980226]{0:T(1024)} reshape(f32[767,1278]{1,0:T(8,128)} %pad.8) | data formatting | bytes 7841808 | tf_op jit(solution)/shard_map/reshape | solution.py:49
  80.8 4.3 %pad.9 = f32[980993]{0:T(1024)} pad(f32[980226]{0:T(1024)} %reshape.66, f32[]{:T(128)} %constant.15.clone.1), padding=0_767 | pad | bytes 7844880 | tf_op jit(solution)/shard_map/jit(_pad)/pad | solution.py:49
  85.0 7.8 %reshape.67 = f32[767,1279]{1,0:T(8,128)} reshape(f32[980993]{0:T(1024)} %pad.9) | data formatting | bytes 7847944 | tf_op jit(solution)/shard_map/reshape | solution.py:50
  92.8 9.2 %fusion = f32[512,1023]{1,0:T(8,128)} fusion(f32[767,1279]{1,0:T(8,128)} %reshape.67, f32[512]{0:T(512)S(1)} %get-tuple-element.6, pred[512]{0:T(512)(128)(4,1)S(1)} %get-tuple-element.15, f32[512]{0:T(512)S(1)} %get-tuple-element.9, pred[512]{0:T(512)(128)(4,1)S(1)} %get-tuple-element.14, pred[512]{0:T(512)(128)(4,1)S(1)} %get-tuple-element.13, ...), kind=kOutput, calls=%fused_computation | convolution fusion | flops 4826332160 | bytes 5250560 | tf_op jit(solution)/shard_map/dot_general | solution.py:51
  102.1 2.9 %reshape.68 = f32[523776]{0:T(1024)S(1)} reshape(f32[512,1023]{1,0:T(8,128)} %fusion) | data formatting | bytes 4190208 | tf_op jit(solution)/shard_map/reshape | solution.py:54
  105.0 2.0 %slice.17 = f32[523264]{0:T(1024)} slice(f32[523776]{0:T(1024)S(1)} %reshape.68), slice={[511:523775]} | slice | bytes 4186112 | tf_op jit(solution)/shard_map/slice | solution.py:54
  106.9 3.4 %reshape.69 = f32[512,1022]{1,0:T(8,128)S(1)} reshape(f32[523264]{0:T(1024)} %slice.17) | data formatting | bytes 4186112 | tf_op jit(solution)/shard_map/reshape | solution.py:55
  110.3 1.1 slice.18
  111.4 0.0 reduce-scatter.2.cloned.1.call-update
  111.4 0.9 broadcast_divide_fusion
  112.3 17.2 %all-reduce.2 = (f32[767]{0:T(1024)S(1)}, f32[767]{0:T(1024)S(1)}) all-reduce(f32[767]{0:T(1024)S(1)} %multiply_reduce_fusion, f32[767]{0:T(1024)S(1)} %multiply_reduce_fusion.1), channel_id=1, replica_groups=mesh['row'=4,'col'=16,'chan'=8] {'chan'}, use_global_device_ids=true, to_apply=%region_7.8 | all-reduce | flops 1534 | bytes 12272 | tf_op jit(solution)/shard_map/psum | solution.py:93
  129.6 0.1 dynamic_slice.26
  129.7 0.3 fusion.18
  129.9 2.5 %fusion.13 = f32[1,512]{1,0:T(1,128)S(1)} fusion(f32[767,1]{0,1:T(1,128)S(1)} %reshape.72, f32[512]{0:T(512)S(1)} %get-tuple-element.5, f32[512]{0:T(512)S(1)} %get-tuple-element.19, s32[512]{0:T(512)S(1)} %get-tuple-element.20, s32[512]{0:T(512)S(1)} %get-tuple-element.21, pred[512]{0:T(512)(128)(4,1)S(1)} %get-tuple-element.17, ...), kind=kOutput, calls=%fused_computation.17 | convolution fusion | flops 10210304 | bytes 14844 | tf_op jit(solution)/shard_map/dot_general | solution.py:101
  132.4 21.2 %reduce-scatter.2.cloned.1.call-done = f32[64,512]{1,0:T(8,128)} async-done(((f32[512,512]{1,0:T(8,128)}), f32[64,512]{1,0:T(8,128)}) %reduce-scatter.2.cloned.1.call-update) | async-done | bytes 131088 | tf_op jit(solution)/shard_map/reduce_scatter | solution.py:87
  153.6 1.7 %divide_exponential_fusion = f32[64,512]{1,0:T(8,128)} fusion(f32[64,512]{1,0:T(8,128)} %reduce-scatter.2.cloned.1.call-done, f32[512]{0:T(512)S(1)} %add_sqrt_fusion, f32[64]{0:T(128)S(1)} %fusion.18), kind=kLoop, calls=%fused_computation.32 | loop fusion | flops 98304 | bytes 264448 | tf_op jit(solution)/shard_map/exp | solution.py:110
  (3 shorter events, 0.0 us)
Async XLA Ops:
  6.5 13.9 %copy-start = (bf16[512,256]{1,0:T(8,128)(2,1)S(1)}, bf16[512,256]{1,0:T(8,128)(2,1)}, u32[]{:S(2)}) copy-start(bf16[512,256]{1,0:T(8,128)(2,1)} %param.4) | copy-start | bytes 786436
  6.5 61.4 %all-gather.2.cloned.1.call-start = ((), (), s32[]{:S(2)}) async-start(), calls=%async_computation.1 | async-start | bytes 6684672 | tf_op jit(solution)/shard_map/all_gather | solution.py:19
  7.5 6.3 %collective-permute-start = (bf16[255,256]{1,0:T(8,128)(2,1)S(1)}, bf16[255,256]{1,0:T(8,128)(2,1)S(1)}, u32[]{:S(2)}, u32[]{:S(2)}) collective-permute-start(bf16[255,256]{1,0:T(8,128)(2,1)S(1)} %slice.12), channel_id=1, source_target_pairs={{120,0},{0,8},{8,16},{16,24},{24,32},{32,40},{40,48},{48,56},{56,6... | collective-permute-start | bytes 391688 | tf_op jit(solution)/shard_map/ppermute | solution.py:14
  15.7 137.9 %reduce-scatter.2.cloned.1.call-start = ((), (), s32[]{:S(2)}) async-start(), calls=%async_computation.2 | async-start | bytes 1179648 | tf_op jit(solution)/shard_map/reduce_scatter | solution.py:87
Sparse Core Ops, SparseCore 0:
  15.8 52.1 all-gather.1
  111.5 42.0 reduce-scatter.1
